TPU v7x, 32 devices: a whole 2x2x4 slice. The times are simulated.
32 devices in a mesh: grp: 8 (over y, x, core), ent: 4 (over z).
Axes of the slice: x: 2, y: 2, z: 4, core: 2. Of those that a mesh axis runs over, the one named last changes fastest.
Arguments:
- factor: bfloat16 [4096, 256], P(('grp', 'ent')), may hold values from -1.5 to 1.5
- cores: bfloat16 [16, 256, 256], replicated, may hold values from -0.375 to 0.375
- adjacency: int32 [768, 128, 128], P(('grp', 'ent')), may hold values 0 or 1
- tile_rels: int32 [32, 24], P(('grp', 'ent')), may hold values from 0 to 15
- tile_count: int32 [32], P(('grp', 'ent')), may hold values from 1 to 24, 480 in all
- send_lists: int32 [32, 4, 6], P(('grp', 'ent')), may hold values from 0 to 7
Outputs:
- factor_grad: float32 [4096, 256], P(('grp', 'ent'))
All inputs are finite; a program needn't handle non-finite values. No bound on the sum of `adjacency` or of `tile_count` on one device may be relied on, other than what follows from the above.
Results may differ from a plain program's by a relative error of at most 0.002.
Values may be sent and summed in bfloat16 or wider, within the bound.
No kernel may reach another device: no remote copies, remote signals or barrier semaphores. Data moves between devices by JAX's collectives and lax.ppermute only.
A program may use at most 64 MiB of HBM per device.

v0:
```python
import jax
import jax.numpy as jnp
from jax import lax
from jax.sharding import PartitionSpec as P

LOSS_SCALE = 0.0625


def on_device(factor, cores, adjacency, tile_rels, tile_count, send_lists):
    ent_count = lax.axis_size("ent")
    grp_count = lax.axis_size("grp")
    my_ent = lax.axis_index("ent")
    tiles = tile_rels.shape[1]
    block = factor.shape[0]
    width = factor.shape[1]
    per_relay = tiles // ent_count
    slots = ent_count * per_relay
    relations = tile_rels[0]
    routes = send_lists[0].reshape(slots)
    group_blocks = lax.all_gather(factor[None], "grp", axis=0, tiled=True)
    outgoing = group_blocks[routes].reshape(ent_count, per_relay, block, width)
    arrived = lax.all_to_all(outgoing, "ent", split_axis=0, concat_axis=0, tiled=True).reshape(
        slots, block, width
    )
    tile_ids = jnp.arange(tiles, dtype=jnp.int32)
    slot_of_tile = (my_ent + tile_ids) % ent_count * per_relay + tile_ids // ent_count
    factor_panels = arrived[slot_of_tile]
    live = (tile_ids < tile_count[0]).astype(jnp.float32)
    by_relation = jnp.einsum(
        "br,krs->kbs", factor, cores, preferred_element_type=jnp.float32
    ).astype(jnp.bfloat16)
    mapped_tiles = by_relation[relations]
    predicted_scores = jnp.einsum(
        "ogj,omj->ogm", mapped_tiles, factor_panels, preferred_element_type=jnp.float32
    )
    score_residual = (
        (predicted_scores - adjacency.astype(jnp.float32)) * (LOSS_SCALE * live)[:, None, None]
    ).astype(jnp.bfloat16)
    relation_product = jnp.einsum(
        "xmw,xwe->xme", score_residual, factor_panels, preferred_element_type=jnp.float32
    ).astype(jnp.bfloat16)
    row_grad = jnp.einsum(
        "tbs,trs->br", relation_product, cores[relations], preferred_element_type=jnp.float32
    )
    slot_ids = jnp.arange(slots, dtype=jnp.int32)
    tile_of_slot = slot_ids % per_relay * ent_count + (slot_ids // per_relay - my_ent) % ent_count
    column_terms = jnp.einsum(
        "yzj,yzh->yjh", score_residual, mapped_tiles, preferred_element_type=jnp.float32
    ).astype(jnp.bfloat16)
    sent_terms = column_terms[tile_of_slot].reshape(ent_count, per_relay, block, width)
    returned = (
        lax.all_to_all(sent_terms, "ent", split_axis=0, concat_axis=0, tiled=True)
        .reshape(slots, block * width)
        .astype(jnp.float32)
    )
    owner_onehot = (routes[:, None] == jnp.arange(grp_count, dtype=jnp.int32)[None, :]).astype(
        jnp.float32
    )
    owner_terms = jnp.dot(
        owner_onehot.T,
        returned,
        precision=lax.Precision.HIGHEST,
        preferred_element_type=jnp.float32,
    )
    owner_part = lax.psum_scatter(
        owner_terms.reshape(grp_count, block, width), "grp", scatter_dimension=0, tiled=True
    )
    return row_grad + owner_part[0]


def solution(mesh):
    in_specs = (
        P(("grp", "ent"), None),
        P(),
        P(("grp", "ent"), None, None),
        P(("grp", "ent"), None),
        P(("grp", "ent")),
        P(("grp", "ent"), None, None),
    )
    out_specs = P(("grp", "ent"), None)
    return jax.shard_map(
        on_device, mesh=mesh, in_specs=in_specs, out_specs=out_specs, check_vma=False
    )
```

profile of v0, /device:TPU:0, one launch (start us, length us, event | category | flops | bytes accessed | tf_op | source)
XLA Modules:
  0.0 166.0 jit_solution(857811333616795226)
XLA Ops:
  6.5 0.0 copy-start
  6.5 0.9 reshape_squeeze.3
  7.5 11.6 %all-gather = bf16[1024,256]{1,0:T(8,128)(2,1)S(1)} all-gather(bf16[128,256]{1,0:T(8,128)(2,1)} %param.6), channel_id=2, replica_groups=mesh['grp'=8,'ent'=4] {'grp'}, dimensions={0}, use_global_device_ids=true | all-gather | bytes 589824 | tf_op jit(solution)/shard_map/all_gather | solution.py:20
  19.1 1.9 %gather_fusion.1 = bf16[24,128,256]{2,1,0:T(8,128)(2,1)} fusion(bf16[8,128,256]{2,1,0:T(8,128)(2,1)S(1)} %bitcast.50, s32[1024]{0:T(1024)S(1)} %pad_clamp_fusion.2), kind=kCustom, calls=%fused_computation.1 | custom fusion | bytes 3145824 | tf_op jit(solution)/shard_map/gather | solution.py:21
  20.9 0.0 copy-start.4
  20.9 0.0 copy-start.2
  20.9 5.0 %all-to-all-start = ((bf16[4,6,128,256]{3,2,1,0:T(8,128)(2,1)}), bf16[4,6,128,256]{3,2,1,0:T(8,128)(2,1)}, u32[]{:S(2)}, u32[]{:S(2)}) async-start(bf16[4,6,128,256]{3,2,1,0:T(8,128)(2,1)} %bitcast.51), calls=%async_computation | async-start | bytes 3145728 | tf_op jit(solution)/shard_map/all_to_all | solution.py:22
  26.6 0.0 copy-done.4
  26.6 0.0 copy-done
  26.6 0.0 copy-done.2
  26.6 0.8 fusion.4
  27.4 1.9 %gather_fusion = bf16[24,128,256]{1,2,0:T(8,128)(2,1)} fusion(bf16[16,128,256]{1,2,0:T(8,128)(2,1)S(1)} %fusion.4, s32[1024]{0:T(1024)S(1)} %pad_clamp_fusion.3), kind=kCustom, calls=%fused_computation | custom fusion | bytes 3145824 | tf_op jit(solution)/shard_map/gather | solution.py:32
  29.4 34.1 %all-to-all-done = bf16[4,6,128,256]{3,2,1,0:T(8,128)(2,1)} async-done(((bf16[4,6,128,256]{3,2,1,0:T(8,128)(2,1)}), bf16[4,6,128,256]{3,2,1,0:T(8,128)(2,1)}, u32[]{:S(2)}, u32[]{:S(2)}) %all-to-all-start) | async-done | bytes 1572896 | tf_op jit(solution)/shard_map/all_to_all | solution.py:22
  63.5 3.3 %gather_fusion.2 = bf16[24,128,256]{2,1,0:T(8,128)(2,1)} fusion(bf16[24,128,256]{2,1,0:T(8,128)(2,1)} %bitcast.7, s32[1024]{0:T(1024)S(1)} %pad_clamp_fusion.1), kind=kCustom, calls=%fused_computation.2 | custom fusion | bytes 3145824 | tf_op jit(solution)/shard_map/gather | solution.py:27
  66.8 0.0 copy-start.1
  66.8 3.2 %multiply_convert_fusion = bf16[24,128,128]{2,1,0:T(8,128)(2,1)S(1)} fusion(s32[24,128,128]{2,1,0:T(8,128)} %param.8, bf16[24,128,256]{1,2,0:T(8,128)(2,1)} %gather_fusion, bf16[24,128,256]{2,1,0:T(8,128)(2,1)} %gather_fusion.2, f32[24]{0:T(128)S(1)} %compare_select_fusion.8), kind=kOutput, calls=%fused_computation.10 | convolution fusion | flops 202899456 | bytes 5505120 | tf_op jit(solution)/shard_map/ogj,omj->ogm/dot_general | solution.py:33
  69.9 0.0 copy-done.1
  70.0 1.8 %convolution_convert_fusion = bf16[24,128,256]{2,1,0:T(8,128)(2,1)} fusion(bf16[24,128,128]{2,1,0:T(8,128)(2,1)S(1)} %multiply_convert_fusion, bf16[24,128,256]{1,2,0:T(8,128)(2,1)S(1)} %copy-done.1), kind=kOutput, calls=%fused_computation.5 | convolution fusion | flops 202113024 | bytes 3932160 | tf_op jit(solution)/shard_map/yzj,yzh->yjh/dot_general | solution.py:47
  71.7 3.2 %gather_fusion.4 = bf16[24,128,256]{2,1,0:T(8,128)(2,1)} fusion(bf16[24,128,256]{2,1,0:T(8,128)(2,1)} %convolution_convert_fusion, s32[1024]{0:T(1024)S(1)} %pad_clamp_fusion), kind=kCustom, calls=%fused_computation.4 | custom fusion | bytes 3145824 | tf_op jit(solution)/shard_map/gather | solution.py:50
  75.0 0.0 copy-start.3
  75.0 4.5 %all-to-all-start.1 = ((bf16[4,6,128,256]{3,2,1,0:T(8,128)(2,1)}), bf16[4,6,128,256]{3,2,1,0:T(8,128)(2,1)}, u32[]{:S(2)}, u32[]{:S(2)}) async-start(bf16[4,6,128,256]{3,2,1,0:T(8,128)(2,1)} %bitcast.52), calls=%async_computation.1 | async-start | bytes 3145728 | tf_op jit(solution)/shard_map/all_to_all | solution.py:52
  79.5 0.0 reduce-scatter.2.cloned.1.call-start
  79.5 0.0 copy-done.3
  79.5 0.1 eq.19
  79.6 36.6 %all-to-all-done.1 = bf16[4,6,128,256]{3,2,1,0:T(8,128)(2,1)} async-done(((bf16[4,6,128,256]{3,2,1,0:T(8,128)(2,1)}), bf16[4,6,128,256]{3,2,1,0:T(8,128)(2,1)}, u32[]{:S(2)}, u32[]{:S(2)}) %all-to-all-start.1) | async-done | bytes 1572896 | tf_op jit(solution)/shard_map/all_to_all | solution.py:52
  116.2 2.6 %fusion = f32[8,128,256]{2,0,1:T(8,128)S(1)} fusion(s32[24]{0:T(128)S(1)} %eq.19, bf16[3,8,128,256]{3,2,1,0:T(8,128)(2,1)} %bitcast.19), kind=kOutput, calls=%fused_computation.7 | convolution fusion | flops 12583104 | bytes 2621536 | tf_op jit(solution)/shard_map/dot_general | solution.py:59
  118.8 1.3 copy.17
  120.2 0.0 reduce-scatter.2.cloned.1.call-update
  120.2 2.5 %gather_fusion.3 = bf16[24,256,256]{2,1,0:T(8,128)(2,1)} fusion(bf16[16,256,256]{2,1,0:T(8,128)(2,1)S(1)} %copy-done, s32[1024]{0:T(1024)S(1)} %pad_clamp_fusion.3), kind=kCustom, calls=%fused_computation.3 | custom fusion | bytes 6291552 | tf_op jit(solution)/shard_map/gather | solution.py:43
  122.7 31.8 %reduce-scatter.2.cloned.1.call-done = f32[1,128,256]{2,1,0:T(8,128)} async-done(((f32[8,128,256]{2,1,0:T(8,128)}), f32[1,128,256]{2,1,0:T(8,128)}) %reduce-scatter.2.cloned.1.call-update) | async-done | bytes 131088 | tf_op jit(solution)/shard_map/reduce_scatter | solution.py:65
  154.5 4.6 %fusion.6 = f32[128,256]{1,0:T(8,128)} fusion(bf16[24,256,256]{2,1,0:T(8,128)(2,1)} %gather_fusion.3, bf16[24,128,128]{2,1,0:T(8,128)(2,1)S(1)} %multiply_convert_fusion, bf16[24,128,256]{2,1,0:T(8,128)(2,1)} %gather_fusion.2, f32[1,128,256]{2,1,0:T(8,128)} %reduce-scatter.2.cloned.1.call-done), kind=kOutput, calls=%fused_computation.15 | convolution fusion | flops 604798976 | bytes 5767168 | tf_op jit(solution)/shard_map/tbs,trs->br/dot_general | solution.py:42
  (9 shorter events, 0.1 us)
Async XLA Ops:
  6.5 20.1 %copy-start = (bf16[16,256,256]{2,1,0:T(8,128)(2,1)S(1)}, bf16[16,256,256]{2,1,0:T(8,128)(2,1)}, u32[]{:S(2)}) copy-start(bf16[16,256,256]{2,1,0:T(8,128)(2,1)} %param.7) | copy-start | bytes 6291460
  20.9 5.7 %copy-start.4 = (s32[1,24]{1,0:T(1,128)S(1)}, s32[1,24]{1,0:T(1,128)}, u32[]{:S(2)}) copy-start(s32[1,24]{1,0:T(1,128)} %param.9) | copy-start | bytes 292
  20.9 5.7 %copy-start.2 = (bf16[128,256]{1,0:T(8,128)(2,1)S(1)}, bf16[128,256]{1,0:T(8,128)(2,1)}, u32[]{:S(2)}) copy-start(bf16[128,256]{1,0:T(8,128)(2,1)} %param.6) | copy-start | bytes 196612
  20.9 42.6 %all-to-all-start = ((bf16[4,6,128,256]{3,2,1,0:T(8,128)(2,1)}), bf16[4,6,128,256]{3,2,1,0:T(8,128)(2,1)}, u32[]{:S(2)}, u32[]{:S(2)}) async-start(bf16[4,6,128,256]{3,2,1,0:T(8,128)(2,1)} %bitcast.51), calls=%async_computation | async-start | bytes 3145728 | tf_op jit(solution)/shard_map/all_to_all | solution.py:22
  66.8 3.2 %copy-start.1 = (bf16[24,128,256]{1,2,0:T(8,128)(2,1)S(1)}, bf16[24,128,256]{1,2,0:T(8,128)(2,1)}, u32[]{:S(2)}) copy-start(bf16[24,128,256]{1,2,0:T(8,128)(2,1)} %gather_fusion) | copy-start | bytes 4718596
  75.0 4.5 %copy-start.3 = (s32[1,4,6]{2,1,0:T(4,128)S(1)}, s32[1,4,6]{2,1,0:T(4,128)}, u32[]{:S(2)}) copy-start(s32[1,4,6]{2,1,0:T(4,128)} %param.11) | copy-start | bytes 292
  75.0 41.2 %all-to-all-start.1 = ((bf16[4,6,128,256]{3,2,1,0:T(8,128)(2,1)}), bf16[4,6,128,256]{3,2,1,0:T(8,128)(2,1)}, u32[]{:S(2)}, u32[]{:S(2)}) async-start(bf16[4,6,128,256]{3,2,1,0:T(8,128)(2,1)} %bitcast.52), calls=%async_computation.1 | async-start | bytes 3145728 | tf_op jit(solution)/shard_map/all_to_all | solution.py:52
  79.5 75.0 %reduce-scatter.2.cloned.1.call-start = ((), (), s32[]{:S(2)}) async-start(), calls=%async_computation.3 | async-start | bytes 1179648 | tf_op jit(solution)/shard_map/reduce_scatter | solution.py:65
Sparse Core Ops, SparseCore 0:
  120.3 34.1 reduce-scatter.1
where the time goes:
time: 166 us
  waiting for transfers between devices  103 us (62%)
  local copies, waits for them, and re-layouts  15.2 us (9%)
  between operations  14.2 us (9%)
  matrix products  12.9 us (8%)
  blocking collectives  11.6 us (7%)
  starting transfers between devices  9.52 us (6%)
    all_to_all x1, waiting for transfers between devices, on_device(): lax.all_to_all(sent_terms, 'ent', split_axis=0, concat_axis=0, tiled=True)  36.6 us
    all_to_all x1, waiting for transfers between devices, on_device(): lax.all_to_all(outgoing, 'ent', split_axis=0, concat_axis=0, tiled=True)  34.1 us
    reduce_scatter x1, waiting for transfers between devices, on_device(): lax.psum_scatter(owner_terms.reshape(grp_count, block, width), 'grp', sca...  31.8 us
    all_gather x1, blocking collectives, on_device(): group_blocks = lax.all_gather(factor[None], 'grp', axis=0, tiled=True)  11.6 us
    all_to_all x1, starting transfers between devices, on_device(): lax.all_to_all(outgoing, 'ent', split_axis=0, concat_axis=0, tiled=True)  5 us
    dot_general x1, matrix products, on_device(): jnp.einsum('tbs,trs->br', relation_product, cores[relations], preferred_e...  4.58 us
    all_to_all x1, starting transfers between devices, on_device(): lax.all_to_all(sent_terms, 'ent', split_axis=0, concat_axis=0, tiled=True)  4.48 us
  transfers between devices with their start and end apart: 3, of which 3 were waited for; matrix products, arithmetic and copies ran while one was open for 3% of the time, Pallas kernels for 0%

commit v1 on v0

--- a/solution.py
+++ b/solution.py
@@ -17,7 +17,12 @@
     slots = ent_count * per_relay
     relations = tile_rels[0]
     routes = send_lists[0].reshape(slots)
-    group_blocks = lax.all_gather(factor[None], "grp", axis=0, tiled=True)
+    ring = [factor[None]]
+    for hop in range(7):
+        ring.append(lax.ppermute(ring[-1], "grp", [(dev, (dev + 1) % 8) for dev in range(8)]))
+    group_blocks = jnp.roll(
+        jnp.concatenate(ring[::-1], axis=0), (lax.axis_index("grp") + 1) * ring[0].shape[0], axis=0
+    )
     outgoing = group_blocks[routes].reshape(ent_count, per_relay, block, width)
     arrived = lax.all_to_all(outgoing, "ent", split_axis=0, concat_axis=0, tiled=True).reshape(
         slots, block, width

time: 166 us -> 185 us (1.11)
  waiting for transfers between devices: 103 us -> 131 us
  blocking collectives: 11.6 us -> 0 us
    ppermute x0 -> x7, waiting for transfers between devices: none -> 31.8 us  [on_device(): lax.ppermute(ring[-1], 'grp', [(dev, (dev + 1) % 8) for dev in range(8)])]
    all_gather x1 -> x0, blocking collectives: 11.6 us -> none  [on_device(): group_blocks = lax.all_gather(factor[None], 'grp', axis=0, tiled=True)]
    all_to_all x1, waiting for transfers between devices: 34.1 us -> 30.5 us  [on_device(): lax.all_to_all(outgoing, 'ent', split_axis=0, concat_axis=0, tiled=True)]
  transfers between devices with their start and end apart: 3 -> 10, of which waited for: 3 -> 10; matrix products, arithmetic and copies ran while one was open for 3% -> 3% of each run, Pallas kernels for 0% -> 0%
where the time goes in v1:
time: 185 us
  waiting for transfers between devices  131 us (71%)
  local copies, waits for them, and re-layouts  16 us (9%)
  between operations  14.3 us (8%)
  matrix products  12.9 us (7%)
  starting transfers between devices  10.7 us (6%)
    all_to_all x1, waiting for transfers between devices, on_device(): lax.all_to_all(sent_terms, 'ent', split_axis=0, concat_axis=0, tiled=True)  36.4 us
    reduce_scatter x1, waiting for transfers between devices, on_device(): lax.psum_scatter(owner_terms.reshape(grp_count, block, width), 'grp', sca...  32.3 us
    ppermute x7, waiting for transfers between devices, on_device(): lax.ppermute(ring[-1], 'grp', [(dev, (dev + 1) % 8) for dev in range(8)])  31.8 us
    all_to_all x1, waiting for transfers between devices, on_device(): lax.all_to_all(outgoing, 'ent', split_axis=0, concat_axis=0, tiled=True)  30.5 us
    all_to_all x1, starting transfers between devices, on_device(): lax.all_to_all(outgoing, 'ent', split_axis=0, concat_axis=0, tiled=True)  5.73 us
    dot_general x1, matrix products, on_device(): jnp.einsum('tbs,trs->br', relation_product, cores[relations], preferred_e...  4.59 us
    all_to_all x1, starting transfers between devices, on_device(): lax.all_to_all(sent_terms, 'ent', split_axis=0, concat_axis=0, tiled=True)  4.49 us
  transfers between devices with their start and end apart: 10, of which 10 were waited for; matrix products, arithmetic and copies ran while one was open for 3% of the time, Pallas kernels for 0%

profile of v1, /device:TPU:0, one launch (start us, length us, event | category | flops | bytes accessed | tf_op | source)
XLA Modules:
  0.0 184.9 jit_solution(7478179014726687567)
XLA Ops:
  6.5 0.0 copy-start
  6.5 0.0 copy-start.2
  6.5 0.5 collective-permute-start
  7.0 5.1 %collective-permute-done = bf16[1,128,256]{2,1,0:T(8,128)(2,1)S(1)} collective-permute-done((bf16[1,128,256]{2,1,0:T(8,128)(2,1)}, bf16[1,128,256]{2,1,0:T(8,128)(2,1)S(1)}, u32[]{:S(2)}, u32[]{:S(2)}) %collective-permute-start) | collective-permute-done | bytes 65568 | tf_op jit(solution)/shard_map/ppermute | solution.py:22
  12.1 0.0 collective-permute-start.1
  12.1 4.6 %collective-permute-done.1 = bf16[1,128,256]{2,1,0:T(8,128)(2,1)S(1)} collective-permute-done((bf16[1,128,256]{2,1,0:T(8,128)(2,1)S(1)}, bf16[1,128,256]{2,1,0:T(8,128)(2,1)S(1)}, u32[]{:S(2)}, u32[]{:S(2)}) %collective-permute-start.1) | collective-permute-done | bytes 65568 | tf_op jit(solution)/shard_map/ppermute | solution.py:22
  16.7 0.0 collective-permute-start.2
  16.7 4.6 %collective-permute-done.2 = bf16[1,128,256]{2,1,0:T(8,128)(2,1)S(1)} collective-permute-done((bf16[1,128,256]{2,1,0:T(8,128)(2,1)S(1)}, bf16[1,128,256]{2,1,0:T(8,128)(2,1)S(1)}, u32[]{:S(2)}, u32[]{:S(2)}) %collective-permute-start.2) | collective-permute-done | bytes 65568 | tf_op jit(solution)/shard_map/ppermute | solution.py:22
  21.2 0.0 collective-permute-start.3
  21.2 0.8 reshape_squeeze.3
  22.0 3.8 %collective-permute-done.3 = bf16[1,128,256]{2,1,0:T(8,128)(2,1)S(1)} collective-permute-done((bf16[1,128,256]{2,1,0:T(8,128)(2,1)S(1)}, bf16[1,128,256]{2,1,0:T(8,128)(2,1)S(1)}, u32[]{:S(2)}, u32[]{:S(2)}) %collective-permute-start.3) | collective-permute-done | bytes 65568 | tf_op jit(solution)/shard_map/ppermute | solution.py:22
  25.8 0.0 collective-permute-start.4
  25.8 4.6 %collective-permute-done.4 = bf16[1,128,256]{2,1,0:T(8,128)(2,1)S(1)} collective-permute-done((bf16[1,128,256]{2,1,0:T(8,128)(2,1)S(1)}, bf16[1,128,256]{2,1,0:T(8,128)(2,1)S(1)}, u32[]{:S(2)}, u32[]{:S(2)}) %collective-permute-start.4) | collective-permute-done | bytes 65568 | tf_op jit(solution)/shard_map/ppermute | solution.py:22
  30.4 0.0 collective-permute-start.5
  30.5 4.6 %collective-permute-done.5 = bf16[1,128,256]{2,1,0:T(8,128)(2,1)S(1)} collective-permute-done((bf16[1,128,256]{2,1,0:T(8,128)(2,1)S(1)}, bf16[1,128,256]{2,1,0:T(8,128)(2,1)S(1)}, u32[]{:S(2)}, u32[]{:S(2)}) %collective-permute-start.5) | collective-permute-done | bytes 65568 | tf_op jit(solution)/shard_map/ppermute | solution.py:22
  35.0 0.0 collective-permute-start.6
  35.0 4.6 %collective-permute-done.6 = bf16[1,128,256]{2,1,0:T(8,128)(2,1)S(1)} collective-permute-done((bf16[1,128,256]{2,1,0:T(8,128)(2,1)S(1)}, bf16[1,128,256]{2,1,0:T(8,128)(2,1)S(1)}, u32[]{:S(2)}, u32[]{:S(2)}) %collective-permute-start.6) | collective-permute-done | bytes 65568 | tf_op jit(solution)/shard_map/ppermute | solution.py:22
  39.7 0.8 constant_dynamic-update-slice_fusion.8
  40.6 0.0 copy-done.2
  40.7 1.9 %gather_fusion.1 = bf16[24,128,256]{2,1,0:T(8,128)(2,1)} fusion(bf16[8,128,256]{2,1,0:T(8,128)(2,1)S(1)} %constant_dynamic-slice_fusion, s32[1024]{0:T(1024)S(1)} %get-tuple-element.6), kind=kCustom, calls=%fused_computation.1 | custom fusion | bytes 3145824 | tf_op jit(solution)/shard_map/gather | solution.py:26
  42.6 0.0 copy-start.4
  42.6 5.7 %all-to-all-start = ((bf16[4,6,128,256]{3,2,1,0:T(8,128)(2,1)}), bf16[4,6,128,256]{3,2,1,0:T(8,128)(2,1)}, u32[]{:S(2)}, u32[]{:S(2)}) async-start(bf16[4,6,128,256]{3,2,1,0:T(8,128)(2,1)} %bitcast.52), calls=%async_computation | async-start | bytes 3145728 | tf_op jit(solution)/shard_map/all_to_all | solution.py:27
  49.0 0.0 copy-done.4
  49.0 0.0 copy-done
  49.0 0.8 fusion.4
  49.8 1.9 %gather_fusion = bf16[24,128,256]{1,2,0:T(8,128)(2,1)} fusion(bf16[16,128,256]{1,2,0:T(8,128)(2,1)S(1)} %fusion.4, s32[1024]{0:T(1024)S(1)} %get-tuple-element.8), kind=kCustom, calls=%fused_computation | custom fusion | bytes 3145824 | tf_op jit(solution)/shard_map/gather | solution.py:37
  51.7 30.5 %all-to-all-done = bf16[4,6,128,256]{3,2,1,0:T(8,128)(2,1)} async-done(((bf16[4,6,128,256]{3,2,1,0:T(8,128)(2,1)}), bf16[4,6,128,256]{3,2,1,0:T(8,128)(2,1)}, u32[]{:S(2)}, u32[]{:S(2)}) %all-to-all-start) | async-done | bytes 1572896 | tf_op jit(solution)/shard_map/all_to_all | solution.py:27
  82.2 3.3 %gather_fusion.2 = bf16[24,128,256]{2,1,0:T(8,128)(2,1)} fusion(bf16[24,128,256]{2,1,0:T(8,128)(2,1)} %bitcast.7, s32[1024]{0:T(1024)S(1)} %get-tuple-element.7), kind=kCustom, calls=%fused_computation.2 | custom fusion | bytes 3145824 | tf_op jit(solution)/shard_map/gather | solution.py:32
  85.5 0.0 copy-start.1
  85.5 3.2 %multiply_convert_fusion = bf16[24,128,128]{2,1,0:T(8,128)(2,1)S(1)} fusion(s32[24,128,128]{2,1,0:T(8,128)} %param.8, bf16[24,128,256]{1,2,0:T(8,128)(2,1)} %gather_fusion, bf16[24,128,256]{2,1,0:T(8,128)(2,1)} %gather_fusion.2, f32[24]{0:T(128)S(1)} %compare_select_fusion.8), kind=kOutput, calls=%fused_computation.10 | convolution fusion | flops 202899456 | bytes 5505120 | tf_op jit(solution)/shard_map/ogj,omj->ogm/dot_general | solution.py:38
  88.6 0.0 copy-done.1
  88.6 1.8 convolution_convert_fusion
  90.4 3.3 %gather_fusion.4 = bf16[24,128,256]{2,1,0:T(8,128)(2,1)} fusion(bf16[24,128,256]{2,1,0:T(8,128)(2,1)} %convolution_convert_fusion, s32[1024]{0:T(1024)S(1)} %get-tuple-element.5), kind=kCustom, calls=%fused_computation.4 | custom fusion | bytes 3145824 | tf_op jit(solution)/shard_map/gather | solution.py:55
  93.7 0.0 copy-start.3
  93.7 4.5 %all-to-all-start.1 = ((bf16[4,6,128,256]{3,2,1,0:T(8,128)(2,1)}), bf16[4,6,128,256]{3,2,1,0:T(8,128)(2,1)}, u32[]{:S(2)}, u32[]{:S(2)}) async-start(bf16[4,6,128,256]{3,2,1,0:T(8,128)(2,1)} %bitcast.53), calls=%async_computation.1 | async-start | bytes 3145728 | tf_op jit(solution)/shard_map/all_to_all | solution.py:57
  98.2 0.0 reduce-scatter.2.cloned.1.call-start
  98.2 0.0 copy-done.3
  98.3 0.1 eq.22
  98.3 36.4 %all-to-all-done.1 = bf16[4,6,128,256]{3,2,1,0:T(8,128)(2,1)} async-done(((bf16[4,6,128,256]{3,2,1,0:T(8,128)(2,1)}), bf16[4,6,128,256]{3,2,1,0:T(8,128)(2,1)}, u32[]{:S(2)}, u32[]{:S(2)}) %all-to-all-start.1) | async-done | bytes 1572896 | tf_op jit(solution)/shard_map/all_to_all | solution.py:57
  134.7 2.6 %fusion = f32[8,128,256]{2,0,1:T(8,128)S(1)} fusion(s32[24]{0:T(128)S(1)} %eq.22, bf16[3,8,128,256]{3,2,1,0:T(8,128)(2,1)} %bitcast.19), kind=kOutput, calls=%fused_computation.7 | convolution fusion | flops 12583104 | bytes 2621536 | tf_op jit(solution)/shard_map/dot_general | solution.py:64
  137.4 1.3 copy.17
  138.7 0.0 reduce-scatter.2.cloned.1.call-update
  138.7 2.5 %gather_fusion.3 = bf16[24,256,256]{2,1,0:T(8,128)(2,1)} fusion(bf16[16,256,256]{2,1,0:T(8,128)(2,1)S(1)} %copy-done, s32[1024]{0:T(1024)S(1)} %get-tuple-element.8), kind=kCustom, calls=%fused_computation.3 | custom fusion | bytes 6291552 | tf_op jit(solution)/shard_map/gather | solution.py:48
  141.2 32.3 %reduce-scatter.2.cloned.1.call-done = f32[1,128,256]{2,1,0:T(8,128)} async-done(((f32[8,128,256]{2,1,0:T(8,128)}), f32[1,128,256]{2,1,0:T(8,128)}) %reduce-scatter.2.cloned.1.call-update) | async-done | bytes 131088 | tf_op jit(solution)/shard_map/reduce_scatter | solution.py:70
  173.5 4.6 %fusion.6 = f32[128,256]{1,0:T(8,128)} fusion(bf16[24,256,256]{2,1,0:T(8,128)(2,1)} %gather_fusion.3, bf16[24,128,128]{2,1,0:T(8,128)(2,1)S(1)} %multiply_convert_fusion, bf16[24,128,256]{2,1,0:T(8,128)(2,1)} %gather_fusion.2, f32[1,128,256]{2,1,0:T(8,128)} %reduce-scatter.2.cloned.1.call-done), kind=kOutput, calls=%fused_computation.15 | convolution fusion | flops 604798976 | bytes 5767168 | tf_op jit(solution)/shard_map/tbs,trs->br/dot_general | solution.py:47
  (23 shorter events, 0.2 us)
Async XLA Ops:
  6.5 42.5 %copy-start = (bf16[16,256,256]{2,1,0:T(8,128)(2,1)S(1)}, bf16[16,256,256]{2,1,0:T(8,128)(2,1)}, u32[]{:S(2)}) copy-start(bf16[16,256,256]{2,1,0:T(8,128)(2,1)} %param.7) | copy-start | bytes 6291460
  6.5 34.1 %copy-start.2 = (bf16[128,256]{1,0:T(8,128)(2,1)S(1)}, bf16[128,256]{1,0:T(8,128)(2,1)}, u32[]{:S(2)}) copy-start(bf16[128,256]{1,0:T(8,128)(2,1)} %param.6) | copy-start | bytes 196612
  6.5 5.5 %collective-permute-start = (bf16[1,128,256]{2,1,0:T(8,128)(2,1)}, bf16[1,128,256]{2,1,0:T(8,128)(2,1)S(1)}, u32[]{:S(2)}, u32[]{:S(2)}) collective-permute-start(bf16[1,128,256]{2,1,0:T(8,128)(2,1)} %bitcast.54), channel_id=1, source_target_pairs={{0,4},{4,8},{8,12},{12,16},{16,20},{20,24},{24,28},{28,0},{1,5},{5... | collective-permute-start | bytes 196616 | tf_op jit(solution)/shard_map/ppermute | solution.py:22
  12.1 4.6 %collective-permute-start.1 = (bf16[1,128,256]{2,1,0:T(8,128)(2,1)S(1)}, bf16[1,128,256]{2,1,0:T(8,128)(2,1)S(1)}, u32[]{:S(2)}, u32[]{:S(2)}) collective-permute-start(bf16[1,128,256]{2,1,0:T(8,128)(2,1)S(1)} %collective-permute-done), channel_id=1, source_target_pairs={{0,4},{4,8},{8,12},{12,16},{16,20},{20,24},{24,28},{28,0},{1,5},{5... | collective-permute-start | bytes 196616 | tf_op jit(solution)/shard_map/ppermute | solution.py:22
  16.7 4.6 %collective-permute-start.2 = (bf16[1,128,256]{2,1,0:T(8,128)(2,1)S(1)}, bf16[1,128,256]{2,1,0:T(8,128)(2,1)S(1)}, u32[]{:S(2)}, u32[]{:S(2)}) collective-permute-start(bf16[1,128,256]{2,1,0:T(8,128)(2,1)S(1)} %collective-permute-done.1), channel_id=1, source_target_pairs={{0,4},{4,8},{8,12},{12,16},{16,20},{20,24},{24,28},{28,0},{1,5},{5... | collective-permute-start | bytes 196616 | tf_op jit(solution)/shard_map/ppermute | solution.py:22
  21.2 4.6 %collective-permute-start.3 = (bf16[1,128,256]{2,1,0:T(8,128)(2,1)S(1)}, bf16[1,128,256]{2,1,0:T(8,128)(2,1)S(1)}, u32[]{:S(2)}, u32[]{:S(2)}) collective-permute-start(bf16[1,128,256]{2,1,0:T(8,128)(2,1)S(1)} %collective-permute-done.2), channel_id=1, source_target_pairs={{0,4},{4,8},{8,12},{12,16},{16,20},{20,24},{24,28},{28,0},{1,5},{5... | collective-permute-start | bytes 196616 | tf_op jit(solution)/shard_map/ppermute | solution.py:22
  25.8 4.6 %collective-permute-start.4 = (bf16[1,128,256]{2,1,0:T(8,128)(2,1)S(1)}, bf16[1,128,256]{2,1,0:T(8,128)(2,1)S(1)}, u32[]{:S(2)}, u32[]{:S(2)}) collective-permute-start(bf16[1,128,256]{2,1,0:T(8,128)(2,1)S(1)} %collective-permute-done.3), channel_id=1, source_target_pairs={{0,4},{4,8},{8,12},{12,16},{16,20},{20,24},{24,28},{28,0},{1,5},{5... | collective-permute-start | bytes 196616 | tf_op jit(solution)/shard_map/ppermute | solution.py:22
  30.4 4.6 %collective-permute-start.5 = (bf16[1,128,256]{2,1,0:T(8,128)(2,1)S(1)}, bf16[1,128,256]{2,1,0:T(8,128)(2,1)S(1)}, u32[]{:S(2)}, u32[]{:S(2)}) collective-permute-start(bf16[1,128,256]{2,1,0:T(8,128)(2,1)S(1)} %collective-permute-done.4), channel_id=1, source_target_pairs={{0,4},{4,8},{8,12},{12,16},{16,20},{20,24},{24,28},{28,0},{1,5},{5... | collective-permute-start | bytes 196616 | tf_op jit(solution)/shard_map/ppermute | solution.py:22
  35.0 4.6 %collective-permute-start.6 = (bf16[1,128,256]{2,1,0:T(8,128)(2,1)S(1)}, bf16[1,128,256]{2,1,0:T(8,128)(2,1)S(1)}, u32[]{:S(2)}, u32[]{:S(2)}) collective-permute-start(bf16[1,128,256]{2,1,0:T(8,128)(2,1)S(1)} %collective-permute-done.5), channel_id=1, source_target_pairs={{0,4},{4,8},{8,12},{12,16},{16,20},{20,24},{24,28},{28,0},{1,5},{5... | collective-permute-start | bytes 196616 | tf_op jit(solution)/shard_map/ppermute | solution.py:22
  42.6 6.4 %copy-start.4 = (s32[1,24]{1,0:T(1,128)S(1)}, s32[1,24]{1,0:T(1,128)}, u32[]{:S(2)}) copy-start(s32[1,24]{1,0:T(1,128)} %param.9) | copy-start | bytes 292
  42.6 39.6 %all-to-all-start = ((bf16[4,6,128,256]{3,2,1,0:T(8,128)(2,1)}), bf16[4,6,128,256]{3,2,1,0:T(8,128)(2,1)}, u32[]{:S(2)}, u32[]{:S(2)}) async-start(bf16[4,6,128,256]{3,2,1,0:T(8,128)(2,1)} %bitcast.52), calls=%async_computation | async-start | bytes 3145728 | tf_op jit(solution)/shard_map/all_to_all | solution.py:27
  85.5 3.2 %copy-start.1 = (bf16[24,128,256]{1,2,0:T(8,128)(2,1)S(1)}, bf16[24,128,256]{1,2,0:T(8,128)(2,1)}, u32[]{:S(2)}) copy-start(bf16[24,128,256]{1,2,0:T(8,128)(2,1)} %gather_fusion) | copy-start | bytes 4718596
  93.7 4.5 %copy-start.3 = (s32[1,4,6]{2,1,0:T(4,128)S(1)}, s32[1,4,6]{2,1,0:T(4,128)}, u32[]{:S(2)}) copy-start(s32[1,4,6]{2,1,0:T(4,128)} %param.11) | copy-start | bytes 292
  93.7 41.0 %all-to-all-start.1 = ((bf16[4,6,128,256]{3,2,1,0:T(8,128)(2,1)}), bf16[4,6,128,256]{3,2,1,0:T(8,128)(2,1)}, u32[]{:S(2)}, u32[]{:S(2)}) async-start(bf16[4,6,128,256]{3,2,1,0:T(8,128)(2,1)} %bitcast.53), calls=%async_computation.1 | async-start | bytes 3145728 | tf_op jit(solution)/shard_map/all_to_all | solution.py:57
  98.2 75.3 %reduce-scatter.2.cloned.1.call-start = ((), (), s32[]{:S(2)}) async-start(), calls=%async_computation.3 | async-start | bytes 1179648 | tf_op jit(solution)/shard_map/reduce_scatter | solution.py:70
Sparse Core Ops, SparseCore 0:
  138.8 34.6 reduce-scatter.1
